TPU v7x, 512 devices: a whole 4x4x16 slice. The times are simulated.
512 devices in a mesh: seq: 128 (over y, z, core), head: 4 (over x).
Axes of the slice: x: 4, y: 4, z: 16, core: 2. Of those that a mesh axis runs over, the one named last changes fastest.
Arguments:
- tokens: bfloat16 [64, 4, 1024], P('head'), may hold values from -6 to 6
- cache_keys: bfloat16 [64, 4096, 512], P(None, 'seq', 'head'), may hold values from -70 to 70
- cache_values: bfloat16 [64, 4096, 512], P(None, 'seq', 'head'), may hold values from -6 to 6
- held_states: bfloat16 [64, 512, 1024], P(None, 'seq'), may hold values from -6 to 6
- recompute_pos: int32 [64, 512], P(None, 'seq'), may hold values from 0 to 4095, as said below
- cache_len: int32 [64], replicated, may hold values from 1 to 4096
- new_prompt: int32 [64], replicated, may hold values 0 or 1
- w_qkv: bfloat16 [3, 1024, 512], P(None, None, 'head'), may hold values from -0.1875 to 0.1875
- qkv_bias: float32 [3, 512], P(None, 'head'), may hold values from -3 to 3
- w_out: bfloat16 [512, 1024], P('head'), may hold values from -1.5 to 1.5
- out_bias: float32 [1024], replicated, may hold values from -3 to 3
- attn_gain: float32 [1024], replicated, may hold values from 0.1 to 1.9
- attn_shift: float32 [1024], replicated, may hold values from -3 to 3
- w_up: bfloat16 [1024, 2048], P(None, 'head'), may hold values from -0.1875 to 0.1875
- up_bias: float32 [2048], P('head'), may hold values from -3 to 3
- w_down: bfloat16 [2048, 1024], P('head'), may hold values from -0.125 to 0.125
- down_bias: float32 [1024], replicated, may hold values from -3 to 3
- ffn_gain: float32 [1024], replicated, may hold values from 0.1 to 1.9
- ffn_shift: float32 [1024], replicated, may hold values from -3 to 3
Outputs:
- layer_out: bfloat16 [64, 4, 1024], P('head')
Inputs may be any that keep to these rules, and one draw needn't show every extreme that they name: `recompute_pos`: columns s * 4 to (s + 1) * 4 - 1 of a row hold distinct positions from s * 32 to (s + 1) * 32 - 1.
All inputs are finite; a program needn't handle non-finite values.
Results may differ from a plain program's by a relative error of at most 0.011.
Values may be sent and summed in bfloat16 or wider, within the bound.
No kernel may reach another device: no remote copies, remote signals or barrier semaphores. Data moves between devices by JAX's collectives and lax.ppermute only.
A program may use at most 192 MiB of HBM per device.

v0:
```python
import jax
import jax.numpy as jnp
from jax import lax
from jax.sharding import PartitionSpec as P

HDIM = 64
NEG = -1e30
EPS = 1e-05


def layer_norm(values, norm_gain, norm_bias):
    center = jnp.mean(values, axis=-1, keepdims=True)
    spread = values - center
    second = jnp.mean(spread * spread, axis=-1, keepdims=True)
    return spread * lax.rsqrt(second + EPS) * norm_gain + norm_bias


def merge_pair(first_part, second_part):
    first_max, first_sum, first_out = first_part
    second_max, second_sum, second_out = second_part
    joint_max = jnp.maximum(first_max, second_max)
    first_scale = jnp.exp(first_max - joint_max)
    second_scale = jnp.exp(second_max - joint_max)
    return (
        joint_max,
        first_sum * first_scale + second_sum * second_scale,
        first_out * first_scale[..., None] + second_out * second_scale[..., None],
    )


def partial_attention(queries, keys_here, values_here, visible):
    scores = jnp.einsum(
        "rthe,rphe->rthp", queries, keys_here, preferred_element_type=jnp.float32
    ) * HDIM ** (-0.5)
    highest = jnp.max(jnp.where(visible, scores, NEG), axis=-1)
    weights = jnp.exp(jnp.where(visible, scores - highest[..., None], NEG)).astype(jnp.bfloat16)
    totals = jnp.sum(weights.astype(jnp.float32), axis=-1)
    blended = jnp.einsum(
        "rthp,rphe->rthe", weights, values_here, preferred_element_type=jnp.float32
    )
    return (highest, totals, blended)


def seq_merge(block_max, block_sum, block_out):
    n_seq = lax.axis_size("seq")
    head_shape = block_out.shape
    lanes = head_shape[-2] * head_shape[-1]
    rows = block_out.size // lanes
    stat_rows = block_max.size // lanes
    out2 = block_out.reshape(rows, lanes)
    top = block_max.reshape(stat_rows, lanes)
    total = block_sum.reshape(stat_rows, lanes)
    width = head_shape[-1]
    step = 1
    while step < n_seq:
        pairs = [(i, i ^ step) for i in range(n_seq)]
        packed = jnp.concatenate([out2, top, total], axis=0)
        other = lax.ppermute(packed, "seq", pairs)
        o_out = other[:rows]
        o_top = other[rows : rows + stat_rows]
        o_total = other[rows + stat_rows :]
        joint = jnp.maximum(top, o_top)
        mine = jnp.exp(top - joint)
        theirs = jnp.exp(o_top - joint)
        total = total * mine + o_total * theirs
        mine_rows = jnp.repeat(mine.reshape(rows, lanes // width), width, axis=1)
        theirs_rows = jnp.repeat(theirs.reshape(rows, lanes // width), width, axis=1)
        out2 = out2 * mine_rows + o_out * theirs_rows
        top = joint
        step *= 2
    return (top.reshape(block_max.shape), total.reshape(block_sum.shape), out2.reshape(head_shape))


def on_device(
    tokens,
    cache_keys,
    cache_values,
    held_states,
    recompute_pos,
    cache_len,
    new_prompt,
    w_qkv,
    qkv_bias,
    w_out,
    out_bias,
    attn_gain,
    attn_shift,
    w_up,
    up_bias,
    w_down,
    down_bias,
    ffn_gain,
    ffn_shift,
):
    local_width = w_qkv.shape[2]
    local_heads = local_width // HDIM
    requests = cache_keys.shape[0]
    block_len = cache_keys.shape[1]
    own_rows = tokens.shape[0]
    steps_count = tokens.shape[1]
    block_rows = lax.all_gather(tokens, "head", axis=0, tiled=True)
    triple = (
        jnp.einsum("rtd,kdc->rtkc", block_rows, w_qkv, preferred_element_type=jnp.float32)
        + qkv_bias
    )
    triple = triple.astype(jnp.bfloat16).reshape(
        block_rows.shape[0], block_rows.shape[1], 3 * local_width
    )
    gathered = jnp.concatenate([triple, block_rows], axis=2)
    head_shape = (requests, steps_count, local_heads, HDIM)
    queries = gathered[:, :, :local_width].reshape(head_shape)
    new_keys = gathered[:, :, local_width : 2 * local_width].reshape(head_shape)
    new_values = gathered[:, :, 2 * local_width : 3 * local_width].reshape(head_shape)
    fresh_keys = (
        jnp.einsum("rjd,dc->rjc", held_states, w_qkv[1], preferred_element_type=jnp.float32)
        + qkv_bias[1]
    ).astype(jnp.bfloat16)
    offset_pos = lax.axis_index("seq") * block_len
    positions = jnp.arange(block_len, dtype=jnp.int32)
    matches = (recompute_pos - offset_pos)[:, :, None] == positions[None, None, :]
    placed = jnp.einsum(
        "rjp,rjc->rpc", matches.astype(jnp.bfloat16), fresh_keys, preferred_element_type=jnp.float32
    ).astype(jnp.bfloat16)
    replaced = jnp.any(matches, axis=1)
    keys_here = jnp.where(replaced[:, :, None], placed, cache_keys).reshape(
        requests, block_len, local_heads, HDIM
    )
    values_here = cache_values.reshape(requests, block_len, local_heads, HDIM)
    visible = ((offset_pos + positions)[None, :] < cache_len[:, None]) & (new_prompt[:, None] == 0)
    block_max, block_sum, block_out = partial_attention(
        queries, keys_here, values_here, visible[:, None, None, :]
    )
    cache_max, cache_sum, cache_out = seq_merge(block_max, block_sum, block_out)
    order_t = jnp.arange(steps_count, dtype=jnp.int32)
    causal = (order_t[:, None] >= order_t[None, :])[None, :, None, :]
    new_max, new_sum, new_out = partial_attention(queries, new_keys, new_values, causal)
    joint_max, joint_sum, joint_out = merge_pair(
        (cache_max, cache_sum, cache_out), (new_max, new_sum, new_out)
    )
    attended = (
        (joint_out / joint_sum[..., None])
        .astype(jnp.bfloat16)
        .reshape(requests, steps_count, local_width)
    )
    head_terms = jnp.einsum("rtc,cd->rtd", attended, w_out, preferred_element_type=jnp.float32)
    summed = lax.psum(head_terms, "head")
    inputs_all = gathered[:, :, 3 * local_width :]
    normed_all = layer_norm(
        inputs_all.astype(jnp.float32) + summed + out_bias, attn_gain, attn_shift
    ).astype(jnp.bfloat16)
    hidden_all = jax.nn.gelu(
        jnp.einsum("rtd,df->rtf", normed_all, w_up, preferred_element_type=jnp.float32) + up_bias,
        approximate=False,
    ).astype(jnp.bfloat16)
    normed = lax.dynamic_slice_in_dim(normed_all, lax.axis_index("head") * own_rows, own_rows, 0)
    reduced = lax.psum_scatter(
        jnp.einsum("rtf,fd->rtd", hidden_all, w_down, preferred_element_type=jnp.float32),
        "head",
        scatter_dimension=0,
        tiled=True,
    )
    return layer_norm(normed.astype(jnp.float32) + reduced + down_bias, ffn_gain, ffn_shift).astype(
        jnp.bfloat16
    )


def solution(mesh):
    placed = (
        P("head", None, None),
        P(None, "seq", "head"),
        P(None, "seq", "head"),
        P(None, "seq", None),
        P(None, "seq"),
        P(),
        P(),
        P(None, None, "head"),
        P(None, "head"),
        P("head", None),
        P(),
        P(),
        P(),
        P(None, "head"),
        P("head"),
        P("head", None),
        P(),
        P(),
        P(),
    )
    return jax.shard_map(
        on_device, mesh=mesh, in_specs=placed, out_specs=P("head", None, None), check_vma=False
    )
```

profile of v0, /device:TPU:8, one launch (start us, length us, event | category | flops | bytes accessed | tf_op | source)
XLA Modules:
  0.0 232.6 jit_solution(7463980318247415298)
XLA Ops:
  6.5 0.8 broadcast_compare_fusion
  7.3 0.7 slice_bitcast_fusion
  8.0 0.7 broadcast_subtract_fusion
  9.0 1.0 copy.122
  10.0 13.1 %all_gather.3 = bf16[64,4,1024]{2,0,1:T(8,128)(2,1)S(1)} all-gather(bf16[16,4,1024]{2,0,1:T(8,128)(2,1)S(1)} %copy.122), channel_id=1, replica_groups=mesh['seq'=128,'head'=4] {'head'}, dimensions={0}, use_global_device_ids=true | all-gather | bytes 655360 | tf_op jit(solution)/shard_map/all_gather | solution.py:101
  24.3 0.8 reshape.249
  25.3 0.7 copy-done.18
  26.1 0.9 fusion
  27.7 1.7 select_reduce_fusion
  32.4 1.9 collective-permute-start
  34.3 1.3 collective-permute-done
  36.4 3.8 %collective-permute-start.1 = (f32[264,128]{1,0:T(8,128)S(1)}, f32[264,128]{1,0:T(8,128)S(1)}, u32[]{:S(2)}, u32[]{:S(2)}) collective-permute-start(f32[264,128]{1,0:T(8,128)S(1)} %pad_maximum_fusion.1), channel_id=1, source_target_pairs={{0,8},{4,12},{8,0},{12,4},{16,24},{20,28},{24,16},{28,20},{32,40},... | collective-permute-start | bytes 405512 | tf_op jit(solution)/shard_map/ppermute | solution.py:58
  40.3 3.9 %collective-permute-done.1 = f32[264,128]{1,0:T(8,128)S(1)} collective-permute-done((f32[264,128]{1,0:T(8,128)S(1)}, f32[264,128]{1,0:T(8,128)S(1)}, u32[]{:S(2)}, u32[]{:S(2)}) %collective-permute-start.1) | collective-permute-done | bytes 135200 | tf_op jit(solution)/shard_map/ppermute | solution.py:58
  44.9 5.2 %collective-permute-start.2 = (f32[264,128]{1,0:T(8,128)S(1)}, f32[264,128]{1,0:T(8,128)S(1)}, u32[]{:S(2)}, u32[]{:S(2)}) collective-permute-start(f32[264,128]{1,0:T(8,128)S(1)} %pad_maximum_fusion.2), channel_id=1, source_target_pairs={{0,16},{4,20},{8,24},{12,28},{16,0},{20,4},{24,8},{28,12},{32,48},... | collective-permute-start | bytes 405512 | tf_op jit(solution)/shard_map/ppermute | solution.py:58
  50.1 6.1 %collective-permute-done.2 = f32[264,128]{1,0:T(8,128)S(1)} collective-permute-done((f32[264,128]{1,0:T(8,128)S(1)}, f32[264,128]{1,0:T(8,128)S(1)}, u32[]{:S(2)}, u32[]{:S(2)}) %collective-permute-start.2) | collective-permute-done | bytes 135200 | tf_op jit(solution)/shard_map/ppermute | solution.py:58
  57.0 9.1 %collective-permute-start.3 = (f32[264,128]{1,0:T(8,128)S(1)}, f32[264,128]{1,0:T(8,128)S(1)}, u32[]{:S(2)}, u32[]{:S(2)}) collective-permute-start(f32[264,128]{1,0:T(8,128)S(1)} %pad_maximum_fusion.3), channel_id=1, source_target_pairs={{0,32},{4,36},{8,40},{12,44},{16,48},{20,52},{24,56},{28,60},{32,0... | collective-permute-start | bytes 405512 | tf_op jit(solution)/shard_map/ppermute | solution.py:58
  66.2 10.2 %collective-permute-done.3 = f32[264,128]{1,0:T(8,128)S(1)} collective-permute-done((f32[264,128]{1,0:T(8,128)S(1)}, f32[264,128]{1,0:T(8,128)S(1)}, u32[]{:S(2)}, u32[]{:S(2)}) %collective-permute-start.3) | collective-permute-done | bytes 135200 | tf_op jit(solution)/shard_map/ppermute | solution.py:58
  77.1 13.6 %collective-permute-start.4 = (f32[264,128]{1,0:T(8,128)S(1)}, f32[264,128]{1,0:T(8,128)S(1)}, u32[]{:S(2)}, u32[]{:S(2)}) collective-permute-start(f32[264,128]{1,0:T(8,128)S(1)} %pad_maximum_fusion.4), channel_id=1, source_target_pairs={{0,64},{4,68},{8,72},{12,76},{16,80},{20,84},{24,88},{28,92},{32,9... | collective-permute-start | bytes 405512 | tf_op jit(solution)/shard_map/ppermute | solution.py:58
  91.0 12.1 %collective-permute-done.4 = f32[264,128]{1,0:T(8,128)S(1)} collective-permute-done((f32[264,128]{1,0:T(8,128)S(1)}, f32[264,128]{1,0:T(8,128)S(1)}, u32[]{:S(2)}, u32[]{:S(2)}) %collective-permute-start.4) | collective-permute-done | bytes 135200 | tf_op jit(solution)/shard_map/ppermute | solution.py:58
  103.9 3.5 %collective-permute-start.5 = (f32[264,128]{1,0:T(8,128)S(1)}, f32[264,128]{1,0:T(8,128)S(1)}, u32[]{:S(2)}, u32[]{:S(2)}) collective-permute-start(f32[264,128]{1,0:T(8,128)S(1)} %pad_maximum_fusion.5), channel_id=1, source_target_pairs={{0,128},{4,132},{8,136},{12,140},{16,144},{20,148},{24,152},{28,15... | collective-permute-start | bytes 405512 | tf_op jit(solution)/shard_map/ppermute | solution.py:58
  107.8 3.3 %collective-permute-done.5 = f32[264,128]{1,0:T(8,128)S(1)} collective-permute-done((f32[264,128]{1,0:T(8,128)S(1)}, f32[264,128]{1,0:T(8,128)S(1)}, u32[]{:S(2)}, u32[]{:S(2)}) %collective-permute-start.5) | collective-permute-done | bytes 135200 | tf_op jit(solution)/shard_map/ppermute | solution.py:58
  111.9 3.9 %collective-permute-start.6 = (f32[264,128]{1,0:T(8,128)S(1)}, f32[264,128]{1,0:T(8,128)S(1)}, u32[]{:S(2)}, u32[]{:S(2)}) collective-permute-start(f32[264,128]{1,0:T(8,128)S(1)} %pad_maximum_fusion.6), channel_id=1, source_target_pairs={{0,256},{4,260},{8,264},{12,268},{16,272},{20,276},{24,280},{28,28... | collective-permute-start | bytes 405512 | tf_op jit(solution)/shard_map/ppermute | solution.py:58
  116.1 4.2 %collective-permute-done.6 = f32[264,128]{1,0:T(8,128)S(1)} collective-permute-done((f32[264,128]{1,0:T(8,128)S(1)}, f32[264,128]{1,0:T(8,128)S(1)}, u32[]{:S(2)}, u32[]{:S(2)}) %collective-permute-start.6) | collective-permute-done | bytes 135200 | tf_op jit(solution)/shard_map/ppermute | solution.py:58
  123.0 0.7 copy-done.6
  123.7 1.3 fusion.29
  125.3 58.1 %all-reduce.2.cloned.1.call-done = f32[64,4,1024]{2,0,1:T(8,128)} async-done(((f32[64,4,1024]{2,0,1:T(8,128)}), f32[64,4,1024]{2,0,1:T(8,128)}) %all-reduce.2.cloned.1.call-update) | async-done | bytes 1048592 | tf_op jit(solution)/shard_map/psum | solution.py:146
  183.4 1.5 fusion.26
  186.3 0.9 copy-done.16
  187.8 2.5 %fusion.9 = f32[64,4,1024]{2,0,1:T(8,128)} fusion(bf16[512,1024]{1,0:T(8,128)(2,1)S(1)} %copy-done, f32[64,4,512]{2,0,1:T(8,128)S(1)} %get-tuple-element.45, u8[64,512]{1,0:T(8,128)(4,1)S(1)} %get-tuple-element.6, u8[64,512]{1,0:T(8,128)(4,1)S(1)} %get-tuple-element.5), kind=kOutput, calls=%fused_computation.16 | convolution fusion | flops 277610496 | bytes 2686976 | tf_op jit(solution)/shard_map/rtf,fd->rtd/dot_general | solution.py:157
  190.3 32.6 %reduce-scatter.2.cloned.1.call-done = f32[16,4,1024]{2,0,1:T(8,128)} async-done(((f32[64,4,1024]{2,0,1:T(8,128)}), f32[16,4,1024]{2,0,1:T(8,128)}) %reduce-scatter.2.cloned.1.call-update) | async-done | bytes 262160 | tf_op jit(solution)/shard_map/reduce_scatter | solution.py:156
  222.9 1.1 fusion.82
  225.0 0.8 copy.180
  (165 shorter events, 16.3 us)
Async XLA Ops:
  6.5 181.2 %copy-start = (bf16[512,1024]{1,0:T(8,128)(2,1)S(1)}, bf16[512,1024]{1,0:T(8,128)(2,1)}, u32[]{:S(2)}) copy-start(bf16[512,1024]{1,0:T(8,128)(2,1)} %param.34) | copy-start | bytes 3145732
  6.5 16.6 %copy-start.3 = (bf16[3,1024,128]{2,1,0:T(8,128)(2,1)S(1)}, bf16[3,1024,128]{2,1,0:T(8,128)(2,1)}, u32[]{:S(2)}) copy-start(bf16[3,1024,128]{2,1,0:T(8,128)(2,1)} %param.26) | copy-start | bytes 2359300
  6.5 176.9 %all-reduce.2.cloned.1.call-start = ((), (), s32[]{:S(2)}) async-start(), calls=%async_computation.1 | async-start | bytes 2097152 | tf_op jit(solution)/shard_map/psum | solution.py:146
  9.9 13.2 %copy-start.14 = (f32[3,128]{1,0:T(4,128)S(1)}, f32[3,128]{1,0:T(4,128)}, u32[]{:S(2)}) copy-start(f32[3,128]{1,0:T(4,128)} %param.27) | copy-start | bytes 4612
  23.5 1.5 copy-start.17
  25.0 1.0 copy-start.18
  27.0 0.7 copy-start.15
  29.4 1.8 copy-start.4
  32.4 3.2 %collective-permute-start = (f32[264,128]{1,0:T(8,128)S(1)}, f32[264,128]{1,0:T(8,128)S(1)}, u32[]{:S(2)}, u32[]{:S(2)}) collective-permute-start(f32[264,128]{1,0:T(8,128)S(1)} %pad_maximum_fusion), channel_id=1, source_target_pairs={{0,4},{4,0},{8,12},{12,8},{16,20},{20,16},{24,28},{28,24},{32,36},... | collective-permute-start | bytes 405512 | tf_op jit(solution)/shard_map/ppermute | solution.py:58
  36.4 7.7 %collective-permute-start.1 = (f32[264,128]{1,0:T(8,128)S(1)}, f32[264,128]{1,0:T(8,128)S(1)}, u32[]{:S(2)}, u32[]{:S(2)}) collective-permute-start(f32[264,128]{1,0:T(8,128)S(1)} %pad_maximum_fusion.1), channel_id=1, source_target_pairs={{0,8},{4,12},{8,0},{12,4},{16,24},{20,28},{24,16},{28,20},{32,40},... | collective-permute-start | bytes 405512 | tf_op jit(solution)/shard_map/ppermute | solution.py:58
  44.9 11.3 %collective-permute-start.2 = (f32[264,128]{1,0:T(8,128)S(1)}, f32[264,128]{1,0:T(8,128)S(1)}, u32[]{:S(2)}, u32[]{:S(2)}) collective-permute-start(f32[264,128]{1,0:T(8,128)S(1)} %pad_maximum_fusion.2), channel_id=1, source_target_pairs={{0,16},{4,20},{8,24},{12,28},{16,0},{20,4},{24,8},{28,12},{32,48},... | collective-permute-start | bytes 405512 | tf_op jit(solution)/shard_map/ppermute | solution.py:58
  56.9 9.1 %copy-start.5 = (bf16[64,4,128]{2,0,1:T(8,128)(2,1)S(1)}, bf16[64,4,128]{2,0,1:T(8,128)(2,1)}, u32[]{:S(2)}) copy-start(bf16[64,4,128]{2,0,1:T(8,128)(2,1)} %get-tuple-element.41) | copy-start | bytes 196612
  57.0 19.4 %collective-permute-start.3 = (f32[264,128]{1,0:T(8,128)S(1)}, f32[264,128]{1,0:T(8,128)S(1)}, u32[]{:S(2)}, u32[]{:S(2)}) collective-permute-start(f32[264,128]{1,0:T(8,128)S(1)} %pad_maximum_fusion.3), channel_id=1, source_target_pairs={{0,32},{4,36},{8,40},{12,44},{16,48},{20,52},{24,56},{28,60},{32,0... | collective-permute-start | bytes 405512 | tf_op jit(solution)/shard_map/ppermute | solution.py:58
  77.1 13.6 %copy-start.7 = (bf16[64,4,2,64]{3,2,0,1:T(2,128)(2,1)S(1)}, bf16[64,4,2,64]{3,2,0,1:T(2,128)(2,1)}, u32[]{:S(2)}) copy-start(bf16[64,4,2,64]{3,2,0,1:T(2,128)(2,1)} %reshape.249) | copy-start | bytes 196612
  77.1 26.0 %collective-permute-start.4 = (f32[264,128]{1,0:T(8,128)S(1)}, f32[264,128]{1,0:T(8,128)S(1)}, u32[]{:S(2)}, u32[]{:S(2)}) collective-permute-start(f32[264,128]{1,0:T(8,128)S(1)} %pad_maximum_fusion.4), channel_id=1, source_target_pairs={{0,64},{4,68},{8,72},{12,76},{16,80},{20,84},{24,88},{28,92},{32,9... | collective-permute-start | bytes 405512 | tf_op jit(solution)/shard_map/ppermute | solution.py:58
  103.9 7.2 %collective-permute-start.5 = (f32[264,128]{1,0:T(8,128)S(1)}, f32[264,128]{1,0:T(8,128)S(1)}, u32[]{:S(2)}, u32[]{:S(2)}) collective-permute-start(f32[264,128]{1,0:T(8,128)S(1)} %pad_maximum_fusion.5), channel_id=1, source_target_pairs={{0,128},{4,132},{8,136},{12,140},{16,144},{20,148},{24,152},{28,15... | collective-permute-start | bytes 405512 | tf_op jit(solution)/shard_map/ppermute | solution.py:58
  111.9 8.4 %collective-permute-start.6 = (f32[264,128]{1,0:T(8,128)S(1)}, f32[264,128]{1,0:T(8,128)S(1)}, u32[]{:S(2)}, u32[]{:S(2)}) collective-permute-start(f32[264,128]{1,0:T(8,128)S(1)} %pad_maximum_fusion.6), channel_id=1, source_target_pairs={{0,256},{4,260},{8,264},{12,268},{16,272},{20,276},{24,280},{28,28... | collective-permute-start | bytes 405512 | tf_op jit(solution)/shard_map/ppermute | solution.py:58
  122.8 1.0 copy-start.6
  125.1 58.4 %copy-start.8 = (f32[1024]{0:T(1024)S(1)}, f32[1024]{0:T(1024)}, u32[]{:S(2)}) copy-start(f32[1024]{0:T(1024)} %param.29) | copy-start | bytes 12292
  125.1 97.8 %reduce-scatter.2.cloned.1.call-start = ((), (), s32[]{:S(2)}) async-start(), calls=%async_computation.2 | async-start | bytes 1310720 | tf_op jit(solution)/shard_map/reduce_scatter | solution.py:156
  183.4 1.5 copy-start.1
  185.0 0.7 copy-start.11
  185.3 0.7 copy-start.10
  186.0 1.2 copy-start.16
  186.0 1.2 copy-start.19
  190.3 32.6 %copy-start.9 = (f32[1024]{0:T(1024)S(1)}, f32[1024]{0:T(1024)}, u32[]{:S(2)}) copy-start(f32[1024]{0:T(1024)} %param.35) | copy-start | bytes 12292
  222.9 1.1 copy-start.2
  222.9 1.4 copy-start.13
  224.2 0.7 copy-start.12
Sparse Core Ops, SparseCore 0:
  125.2 58.1 all-reduce.1
  190.4 32.4 reduce-scatter.1
where the time goes:
time: 233 us
  waiting for transfers between devices  132 us (57%)
  starting transfers between devices  41.2 us (18%)
  local copies, waits for them, and re-layouts  16.8 us (7%)
  between operations  14.3 us (6%)
  blocking collectives  13.1 us (6%)
  matrix products  8.92 us (4%)
  other arithmetic  6.39 us (3%)
    psum x1, waiting for transfers between devices, on_device(): summed = lax.psum(head_terms, 'head')  58.1 us
    ppermute x7, waiting for transfers between devices, seq_merge(): other = lax.ppermute(packed, 'seq', pairs)  41.2 us
    ppermute x7, starting transfers between devices, seq_merge(): other = lax.ppermute(packed, 'seq', pairs)  41 us
    reduce_scatter x1, waiting for transfers between devices, on_device(): lax.psum_scatter(jnp.einsum('rtf,fd->rtd', hidden_all, w_down, preferred_...  32.6 us
    all_gather x1, blocking collectives, on_device(): block_rows = lax.all_gather(tokens, 'head', axis=0, tiled=True)  13.1 us
    unnamed x41, local copies, waits for them, and re-layouts  4.99 us
  transfers between devices with their start and end apart: 9, of which 9 were waited for; matrix products, arithmetic and copies ran while one was open for 0% of the time, Pallas kernels for 0%

commit v1 on v0

--- a/solution.py
+++ b/solution.py
@@ -6,6 +6,18 @@
 HDIM = 64
 NEG = -1e30
 EPS = 1e-05
+
+
+def cut_the_kinds(point, link_axis, join_dim):
+    return jnp.concatenate(
+        lax.all_to_all(
+            jnp.stack(tuple((point for _ in range(lax.axis_size(link_axis))))),
+            axis_name=link_axis,
+            split_axis=0,
+            concat_axis=0,
+        ),
+        axis=join_dim,
+    )
 
 
 def layer_norm(values, norm_gain, norm_bias):
@@ -98,7 +110,7 @@
     block_len = cache_keys.shape[1]
     own_rows = tokens.shape[0]
     steps_count = tokens.shape[1]
-    block_rows = lax.all_gather(tokens, "head", axis=0, tiled=True)
+    block_rows = cut_the_kinds(tokens, "head", 0)
     triple = (
         jnp.einsum("rtd,kdc->rtkc", block_rows, w_qkv, preferred_element_type=jnp.float32)
         + qkv_bias

time: 233 us -> 228 us (0.979)
  blocking collectives: 13.1 us -> 0 us
  starting transfers between devices: 41.2 us -> 45.3 us
  matrix products: 8.92 us -> 11.4 us
    all_gather x1 -> x0, blocking collectives: 13.1 us -> none  [on_device(): block_rows = lax.all_gather(tokens, 'head', axis=0, tiled=True)]
    all_to_all x0 -> x1, starting transfers between devices: none -> 4.42 us  [cut_the_kinds(): lax.all_to_all(jnp.stack(tuple((point for _ in range(lax.axis_size(link_a...]
    all_to_all x0 -> x1, waiting for transfers between devices: none -> 2.73 us  [cut_the_kinds(): lax.all_to_all(jnp.stack(tuple((point for _ in range(lax.axis_size(link_a...]
    unnamed x41 -> x39, local copies, waits for them, and re-layouts: 4.99 us -> 6.32 us
  transfers between devices with their start and end apart: 9 -> 10, of which waited for: 9 -> 10; matrix products, arithmetic and copies ran while one was open for 0% -> 2% of each run, Pallas kernels for 0% -> 0%
where the time goes in v1:
time: 228 us; the launch traced here: 227 us
  waiting for transfers between devices  133 us (58%)
  starting transfers between devices  45.3 us (20%)
  local copies, waits for them, and re-layouts  18.1 us (8%)
  between operations  14.2 us (6%)
  matrix products  11.4 us (5%)
  other arithmetic  4.88 us (2%)
    psum x1, waiting for transfers between devices, on_device(): summed = lax.psum(head_terms, 'head')  56.7 us
    ppermute x7, waiting for transfers between devices, seq_merge(): other = lax.ppermute(packed, 'seq', pairs)  41.1 us
    ppermute x7, starting transfers between devices, seq_merge(): other = lax.ppermute(packed, 'seq', pairs)  40.6 us
    reduce_scatter x1, waiting for transfers between devices, on_device(): lax.psum_scatter(jnp.einsum('rtf,fd->rtd', hidden_all, w_down, preferred_...  32.6 us
    unnamed x39, local copies, waits for them, and re-layouts  6.32 us
  transfers between devices with their start and end apart: 10, of which 10 were waited for; matrix products, arithmetic and copies ran while one was open for 2% of the time, Pallas kernels for 0%

profile of v1, /device:TPU:8, one launch (start us, length us, event | category | flops | bytes accessed | tf_op | source)
XLA Modules:
  0.0 227.0 jit_solution(13343844990313190711)
XLA Ops:
  6.5 1.0 copy.123
  7.6 0.9 stack.2
  8.5 4.4 %all-to-all-start = ((bf16[4,16,4,1024]{3,1,2,0:T(8,128)(2,1)}), bf16[4,16,4,1024]{3,1,2,0:T(8,128)(2,1)S(1)}, u32[]{:S(2)}, u32[]{:S(2)}) async-start(bf16[4,16,4,1024]{3,1,2,0:T(8,128)(2,1)} %stack.2), calls=%async_computation | async-start | bytes 1048576 | tf_op jit(solution)/shard_map/all_to_all | solution.py:13
  14.6 1.3 fusion.8
  15.9 0.9 fusion
  16.8 1.4 reshape.253
  19.6 2.7 %all-to-all-done = bf16[4,16,4,1024]{3,1,2,0:T(8,128)(2,1)S(1)} async-done(((bf16[4,16,4,1024]{3,1,2,0:T(8,128)(2,1)}), bf16[4,16,4,1024]{3,1,2,0:T(8,128)(2,1)S(1)}, u32[]{:S(2)}, u32[]{:S(2)}) %all-to-all-start) | async-done | bytes 524320 | tf_op jit(solution)/shard_map/all_to_all | solution.py:13
  22.4 1.6 fusion.7
  24.2 2.0 select_reduce_fusion
  28.7 1.9 collective-permute-start
  30.7 1.3 collective-permute-done
  32.7 3.8 %collective-permute-start.1 = (f32[264,128]{1,0:T(8,128)S(1)}, f32[264,128]{1,0:T(8,128)S(1)}, u32[]{:S(2)}, u32[]{:S(2)}) collective-permute-start(f32[264,128]{1,0:T(8,128)S(1)} %pad_maximum_fusion.1), channel_id=1, source_target_pairs={{0,8},{4,12},{8,0},{12,4},{16,24},{20,28},{24,16},{28,20},{32,40},... | collective-permute-start | bytes 405512 | tf_op jit(solution)/shard_map/ppermute | solution.py:70
  36.6 3.9 %collective-permute-done.1 = f32[264,128]{1,0:T(8,128)S(1)} collective-permute-done((f32[264,128]{1,0:T(8,128)S(1)}, f32[264,128]{1,0:T(8,128)S(1)}, u32[]{:S(2)}, u32[]{:S(2)}) %collective-permute-start.1) | collective-permute-done | bytes 135200 | tf_op jit(solution)/shard_map/ppermute | solution.py:70
  41.2 5.2 %collective-permute-start.2 = (f32[264,128]{1,0:T(8,128)S(1)}, f32[264,128]{1,0:T(8,128)S(1)}, u32[]{:S(2)}, u32[]{:S(2)}) collective-permute-start(f32[264,128]{1,0:T(8,128)S(1)} %pad_maximum_fusion.2), channel_id=1, source_target_pairs={{0,16},{4,20},{8,24},{12,28},{16,0},{20,4},{24,8},{28,12},{32,48},... | collective-permute-start | bytes 405512 | tf_op jit(solution)/shard_map/ppermute | solution.py:70
  46.4 6.1 %collective-permute-done.2 = f32[264,128]{1,0:T(8,128)S(1)} collective-permute-done((f32[264,128]{1,0:T(8,128)S(1)}, f32[264,128]{1,0:T(8,128)S(1)}, u32[]{:S(2)}, u32[]{:S(2)}) %collective-permute-start.2) | collective-permute-done | bytes 135200 | tf_op jit(solution)/shard_map/ppermute | solution.py:70
  53.3 9.1 %collective-permute-start.3 = (f32[264,128]{1,0:T(8,128)S(1)}, f32[264,128]{1,0:T(8,128)S(1)}, u32[]{:S(2)}, u32[]{:S(2)}) collective-permute-start(f32[264,128]{1,0:T(8,128)S(1)} %pad_maximum_fusion.3), channel_id=1, source_target_pairs={{0,32},{4,36},{8,40},{12,44},{16,48},{20,52},{24,56},{28,60},{32,0... | collective-permute-start | bytes 405512 | tf_op jit(solution)/shard_map/ppermute | solution.py:70
  62.4 10.3 %collective-permute-done.3 = f32[264,128]{1,0:T(8,128)S(1)} collective-permute-done((f32[264,128]{1,0:T(8,128)S(1)}, f32[264,128]{1,0:T(8,128)S(1)}, u32[]{:S(2)}, u32[]{:S(2)}) %collective-permute-start.3) | collective-permute-done | bytes 135200 | tf_op jit(solution)/shard_map/ppermute | solution.py:70
  73.4 13.4 %collective-permute-start.4 = (f32[264,128]{1,0:T(8,128)S(1)}, f32[264,128]{1,0:T(8,128)S(1)}, u32[]{:S(2)}, u32[]{:S(2)}) collective-permute-start(f32[264,128]{1,0:T(8,128)S(1)} %pad_maximum_fusion.4), channel_id=1, source_target_pairs={{0,64},{4,68},{8,72},{12,76},{16,80},{20,84},{24,88},{28,92},{32,9... | collective-permute-start | bytes 405512 | tf_op jit(solution)/shard_map/ppermute | solution.py:70
  87.0 12.3 %collective-permute-done.4 = f32[264,128]{1,0:T(8,128)S(1)} collective-permute-done((f32[264,128]{1,0:T(8,128)S(1)}, f32[264,128]{1,0:T(8,128)S(1)}, u32[]{:S(2)}, u32[]{:S(2)}) %collective-permute-start.4) | collective-permute-done | bytes 135200 | tf_op jit(solution)/shard_map/ppermute | solution.py:70
  100.1 3.0 %collective-permute-start.5 = (f32[264,128]{1,0:T(8,128)S(1)}, f32[264,128]{1,0:T(8,128)S(1)}, u32[]{:S(2)}, u32[]{:S(2)}) collective-permute-start(f32[264,128]{1,0:T(8,128)S(1)} %pad_maximum_fusion.5), channel_id=1, source_target_pairs={{0,128},{4,132},{8,136},{12,140},{16,144},{20,148},{24,152},{28,15... | collective-permute-start | bytes 405512 | tf_op jit(solution)/shard_map/ppermute | solution.py:70
  103.7 3.3 %collective-permute-done.5 = f32[264,128]{1,0:T(8,128)S(1)} collective-permute-done((f32[264,128]{1,0:T(8,128)S(1)}, f32[264,128]{1,0:T(8,128)S(1)}, u32[]{:S(2)}, u32[]{:S(2)}) %collective-permute-start.5) | collective-permute-done | bytes 135200 | tf_op jit(solution)/shard_map/ppermute | solution.py:70
  107.7 4.2 %collective-permute-start.6 = (f32[264,128]{1,0:T(8,128)S(1)}, f32[264,128]{1,0:T(8,128)S(1)}, u32[]{:S(2)}, u32[]{:S(2)}) collective-permute-start(f32[264,128]{1,0:T(8,128)S(1)} %pad_maximum_fusion.6), channel_id=1, source_target_pairs={{0,256},{4,260},{8,264},{12,268},{16,272},{20,276},{24,280},{28,28... | collective-permute-start | bytes 405512 | tf_op jit(solution)/shard_map/ppermute | solution.py:70
  112.2 3.9 %collective-permute-done.6 = f32[264,128]{1,0:T(8,128)S(1)} collective-permute-done((f32[264,128]{1,0:T(8,128)S(1)}, f32[264,128]{1,0:T(8,128)S(1)}, u32[]{:S(2)}, u32[]{:S(2)}) %collective-permute-start.6) | collective-permute-done | bytes 135200 | tf_op jit(solution)/shard_map/ppermute | solution.py:70
  118.9 0.7 copy-done.4
  119.6 1.3 fusion.28
  121.1 56.7 %all-reduce.2.cloned.1.call-done = f32[64,4,1024]{2,0,1:T(8,128)} async-done(((f32[64,4,1024]{2,0,1:T(8,128)}), f32[64,4,1024]{2,0,1:T(8,128)}) %all-reduce.2.cloned.1.call-update) | async-done | bytes 1048592 | tf_op jit(solution)/shard_map/psum | solution.py:158
  177.8 1.5 fusion.25
  180.7 0.9 copy-done.14
  182.2 2.5 %fusion.9 = f32[64,4,1024]{2,0,1:T(8,128)} fusion(bf16[512,1024]{1,0:T(8,128)(2,1)S(1)} %copy-done, f32[64,4,512]{2,0,1:T(8,128)S(1)} %get-tuple-element.45, u8[64,512]{1,0:T(8,128)(4,1)S(1)} %get-tuple-element.6, u8[64,512]{1,0:T(8,128)(4,1)S(1)} %get-tuple-element.5), kind=kOutput, calls=%fused_computation.16 | convolution fusion | flops 277610496 | bytes 2686976 | tf_op jit(solution)/shard_map/rtf,fd->rtd/dot_general | solution.py:169
  184.7 32.6 %reduce-scatter.2.cloned.1.call-done = f32[16,4,1024]{2,0,1:T(8,128)} async-done(((f32[64,4,1024]{2,0,1:T(8,128)}), f32[16,4,1024]{2,0,1:T(8,128)}) %reduce-scatter.2.cloned.1.call-update) | async-done | bytes 262160 | tf_op jit(solution)/shard_map/reduce_scatter | solution.py:168
  217.3 1.1 fusion.81
  219.4 0.8 copy.182
  (166 shorter events, 16.7 us)
Async XLA Ops:
  6.5 175.6 %copy-start = (bf16[512,1024]{1,0:T(8,128)(2,1)S(1)}, bf16[512,1024]{1,0:T(8,128)(2,1)}, u32[]{:S(2)}) copy-start(bf16[512,1024]{1,0:T(8,128)(2,1)} %param.34) | copy-start | bytes 3145732
  8.4 6.1 %copy-start.15 = (bf16[64,4,1024]{2,1,0:T(4,128)(2,1)S(1)}, bf16[64,4,1024]{2,1,0:T(4,128)(2,1)}, u32[]{:S(2)}) copy-start(bf16[64,4,1024]{2,1,0:T(4,128)(2,1)} %param.22) | copy-start | bytes 1572868
  8.5 13.9 %all-to-all-start = ((bf16[4,16,4,1024]{3,1,2,0:T(8,128)(2,1)}), bf16[4,16,4,1024]{3,1,2,0:T(8,128)(2,1)S(1)}, u32[]{:S(2)}, u32[]{:S(2)}) async-start(bf16[4,16,4,1024]{3,1,2,0:T(8,128)(2,1)} %stack.2), calls=%async_computation | async-start | bytes 1048576 | tf_op jit(solution)/shard_map/all_to_all | solution.py:13
  12.9 164.9 %all-reduce.2.cloned.1.call-start = ((), (), s32[]{:S(2)}) async-start(), calls=%async_computation.2 | async-start | bytes 2097152 | tf_op jit(solution)/shard_map/psum | solution.py:158
  12.9 0.7 copy-start.11
  13.6 0.7 copy-start.12
  14.5 1.3 copy-start.16
  16.8 1.4 copy-start.3
  18.2 0.7 copy-start.18
  18.9 0.7 copy-start.13
  28.7 3.2 %collective-permute-start = (f32[264,128]{1,0:T(8,128)S(1)}, f32[264,128]{1,0:T(8,128)S(1)}, u32[]{:S(2)}, u32[]{:S(2)}) collective-permute-start(f32[264,128]{1,0:T(8,128)S(1)} %pad_maximum_fusion), channel_id=1, source_target_pairs={{0,4},{4,0},{8,12},{12,8},{16,20},{20,16},{24,28},{28,24},{32,36},... | collective-permute-start | bytes 405512 | tf_op jit(solution)/shard_map/ppermute | solution.py:70
  32.7 7.7 %collective-permute-start.1 = (f32[264,128]{1,0:T(8,128)S(1)}, f32[264,128]{1,0:T(8,128)S(1)}, u32[]{:S(2)}, u32[]{:S(2)}) collective-permute-start(f32[264,128]{1,0:T(8,128)S(1)} %pad_maximum_fusion.1), channel_id=1, source_target_pairs={{0,8},{4,12},{8,0},{12,4},{16,24},{20,28},{24,16},{28,20},{32,40},... | collective-permute-start | bytes 405512 | tf_op jit(solution)/shard_map/ppermute | solution.py:70
  41.2 11.3 %collective-permute-start.2 = (f32[264,128]{1,0:T(8,128)S(1)}, f32[264,128]{1,0:T(8,128)S(1)}, u32[]{:S(2)}, u32[]{:S(2)}) collective-permute-start(f32[264,128]{1,0:T(8,128)S(1)} %pad_maximum_fusion.2), channel_id=1, source_target_pairs={{0,16},{4,20},{8,24},{12,28},{16,0},{20,4},{24,8},{28,12},{32,48},... | collective-permute-start | bytes 405512 | tf_op jit(solution)/shard_map/ppermute | solution.py:70
  53.3 19.4 %collective-permute-start.3 = (f32[264,128]{1,0:T(8,128)S(1)}, f32[264,128]{1,0:T(8,128)S(1)}, u32[]{:S(2)}, u32[]{:S(2)}) collective-permute-start(f32[264,128]{1,0:T(8,128)S(1)} %pad_maximum_fusion.3), channel_id=1, source_target_pairs={{0,32},{4,36},{8,40},{12,44},{16,48},{20,52},{24,56},{28,60},{32,0... | collective-permute-start | bytes 405512 | tf_op jit(solution)/shard_map/ppermute | solution.py:70
  73.4 25.9 %collective-permute-start.4 = (f32[264,128]{1,0:T(8,128)S(1)}, f32[264,128]{1,0:T(8,128)S(1)}, u32[]{:S(2)}, u32[]{:S(2)}) collective-permute-start(f32[264,128]{1,0:T(8,128)S(1)} %pad_maximum_fusion.4), channel_id=1, source_target_pairs={{0,64},{4,68},{8,72},{12,76},{16,80},{20,84},{24,88},{28,92},{32,9... | collective-permute-start | bytes 405512 | tf_op jit(solution)/shard_map/ppermute | solution.py:70
  100.1 6.9 %collective-permute-start.5 = (f32[264,128]{1,0:T(8,128)S(1)}, f32[264,128]{1,0:T(8,128)S(1)}, u32[]{:S(2)}, u32[]{:S(2)}) collective-permute-start(f32[264,128]{1,0:T(8,128)S(1)} %pad_maximum_fusion.5), channel_id=1, source_target_pairs={{0,128},{4,132},{8,136},{12,140},{16,144},{20,148},{24,152},{28,15... | collective-permute-start | bytes 405512 | tf_op jit(solution)/shard_map/ppermute | solution.py:70
  107.7 8.4 %collective-permute-start.6 = (f32[264,128]{1,0:T(8,128)S(1)}, f32[264,128]{1,0:T(8,128)S(1)}, u32[]{:S(2)}, u32[]{:S(2)}) collective-permute-start(f32[264,128]{1,0:T(8,128)S(1)} %pad_maximum_fusion.6), channel_id=1, source_target_pairs={{0,256},{4,260},{8,264},{12,268},{16,272},{20,276},{24,280},{28,28... | collective-permute-start | bytes 405512 | tf_op jit(solution)/shard_map/ppermute | solution.py:70
  118.6 1.0 copy-start.4
  120.9 56.9 %copy-start.5 = (f32[1024]{0:T(1024)S(1)}, f32[1024]{0:T(1024)}, u32[]{:S(2)}) copy-start(f32[1024]{0:T(1024)} %param.29) | copy-start | bytes 12292
  120.9 96.4 %reduce-scatter.2.cloned.1.call-start = ((), (), s32[]{:S(2)}) async-start(), calls=%async_computation.3 | async-start | bytes 1310720 | tf_op jit(solution)/shard_map/reduce_scatter | solution.py:168
  177.8 1.5 copy-start.1
  179.4 0.7 copy-start.8
  179.7 0.7 copy-start.7
  180.4 1.2 copy-start.14
  180.4 1.2 copy-start.17
  184.7 32.6 %copy-start.6 = (f32[1024]{0:T(1024)S(1)}, f32[1024]{0:T(1024)}, u32[]{:S(2)}) copy-start(f32[1024]{0:T(1024)} %param.35) | copy-start | bytes 12292
  217.3 1.1 copy-start.2
  217.3 1.4 copy-start.10
  218.6 0.7 copy-start.9
Sparse Core Ops, SparseCore 0:
  121.0 56.7 all-reduce.1
  184.8 32.4 reduce-scatter.1
